TPU v7x, 32 devices: a whole 2x2x4 slice. The times are simulated.
32 devices in a mesh: groups: 2 (over y), rows: 4 (over x, core), rep: 4 (over z).
Axes of the slice: x: 2, y: 2, z: 4, core: 2. Of those that a mesh axis runs over, the one named last changes fastest.
Arguments:
- images: bfloat16 [8, 64, 128, 256], P(('groups', 'rep'), 'rows'), parts along dimension 0, may hold values from -6 to 6
- cotangent: bfloat16 [8, 64, 128, 256], P(('groups', 'rep'), 'rows'), parts along dimension 0, may hold values from -6 to 6
- row_taps: float32 [102, 256], P('groups'), parts along dimension 0, may hold values from -0.875 to 0.875
- col_taps: float32 [102, 256], P('groups'), parts along dimension 0, may hold values from -0.875 to 0.875
- norm_gain: float32 [512], P('groups'), parts along dimension 0, may hold values from 0.25 to 1.75
- norm_shift: float32 [512], P('groups'), parts along dimension 0, may hold values from -3 to 3
- up_weight: bfloat16 [512, 1024], P('groups'), parts along dimension 0, may hold values from -0.375 to 0.375
- up_bias: float32 [2048], P('groups'), parts along dimension 0, may hold values from -3 to 3
- down_weight: bfloat16 [2048, 256], P('groups'), parts along dimension 0, may hold values from -0.1875 to 0.1875
- down_bias: float32 [512], P('groups'), parts along dimension 0, may hold values from -3 to 3
- layer_scale: float32 [512], P('groups'), parts along dimension 0, may hold values from 0.5 to 1.5
Outputs:
- block_out: bfloat16 [8, 64, 128, 256], P(('groups', 'rep'), 'rows'), parts along dimension 0
- image_grad: bfloat16 [8, 64, 128, 256], P(('groups', 'rep'), 'rows'), parts along dimension 0
- row_taps_grad: float32 [102, 256], P('groups'), parts along dimension 0
- col_taps_grad: float32 [102, 256], P('groups'), parts along dimension 0
- scale_grad: float32 [512], P('groups'), parts along dimension 0
- down_bias_grad: float32 [512], P('groups'), parts along dimension 0
- down_grad: float32 [2048, 256], P('groups'), parts along dimension 0
- up_bias_grad: float32 [2048], P('groups'), parts along dimension 0
- up_grad: float32 [512, 1024], P('groups'), parts along dimension 0
- gain_grad: float32 [512], P('groups'), parts along dimension 0
- shift_grad: float32 [512], P('groups'), parts along dimension 0
There are 2 independent parts, one for each index of `groups`. A program takes and returns all parts, laid end to end along the dimension named above; each array names one. Nothing has to cross between parts.
All inputs are finite; a program needn't handle non-finite values.
Results may differ from a plain program's by a relative error of at most 0.0086.
Values may be sent and summed in bfloat16 or wider, within the bound.
No kernel may reach another device: no remote copies, remote signals or barrier semaphores. Data moves between devices by JAX's collectives and lax.ppermute only.
A program may use at most 64 MiB of HBM per device.

v0:
```python
import math
import jax
import jax.numpy as jnp
from jax import lax
from jax.sharding import PartitionSpec as P

EPSILON = 1e-06
CUBIC_TERM = 0.044715
TANH_SCALE = 0.7978845608028654


def activate(pre_act):
    return (
        0.5
        * pre_act
        * (1.0 + jnp.tanh(TANH_SCALE * (pre_act + CUBIC_TERM * pre_act * pre_act * pre_act)))
    )


def activate_slope(pre_act):
    inner = jnp.tanh(TANH_SCALE * (pre_act + CUBIC_TERM * pre_act * pre_act * pre_act))
    return 0.5 * (1.0 + inner) + 0.5 * pre_act * (1.0 - inner * inner) * TANH_SCALE * (
        1.0 + 3.0 * CUBIC_TERM * pre_act * pre_act
    )


def pad_along(source, direction, half_reach):
    widths = [(0, 0)] * source.ndim
    widths[direction] = (half_reach, half_reach)
    return jnp.pad(source, widths)


def slide_padded(padded, taps_table, direction, length):
    shape_out = padded.shape[:direction] + (length,) + padded.shape[direction + 1 :]
    result = jnp.zeros(shape_out, jnp.float32)
    for offset in range(taps_table.shape[0]):
        result = result + taps_table[offset] * lax.slice_in_dim(
            padded, offset, offset + length, axis=direction
        ).astype(jnp.float32)
    return result


def tap_sums(cot_field, padded, taps_count, direction):
    length = cot_field.shape[direction]
    lead_axes = tuple(range(cot_field.ndim - 1))
    return jnp.stack(
        [
            jnp.sum(
                cot_field.astype(jnp.float32)
                * lax.slice_in_dim(padded, offset, offset + length, axis=direction).astype(
                    jnp.float32
                ),
                axis=lead_axes,
            )
            for offset in range(taps_count)
        ]
    )


def pointwise(
    mix_rows,
    image_rows,
    cot_rows,
    norm_gain,
    norm_shift,
    up_weight,
    up_bias,
    down_weight,
    down_bias,
    layer_scale,
):
    mix_float = mix_rows.astype(jnp.float32)
    centered = mix_float - jnp.mean(mix_float, axis=-1, keepdims=True)
    inv_dev = lax.rsqrt(jnp.mean(centered * centered, axis=-1, keepdims=True) + EPSILON)
    standardized = centered * inv_dev
    normed = (standardized * norm_gain + norm_shift).astype(jnp.bfloat16)
    pre_act = jnp.dot(normed, up_weight, preferred_element_type=jnp.float32) + up_bias
    activated = activate(pre_act).astype(jnp.bfloat16)
    branch = jnp.dot(activated, down_weight, preferred_element_type=jnp.float32) + down_bias
    cot_float = cot_rows.astype(jnp.float32)
    block_rows = (image_rows.astype(jnp.float32) + layer_scale * branch).astype(jnp.bfloat16)
    branch_cot = cot_float * layer_scale
    branch_grad = branch_cot.astype(jnp.bfloat16)
    act_cot = lax.dot_general(
        branch_grad, down_weight, (((1,), (1,)), ((), ())), preferred_element_type=jnp.float32
    )
    pre_cot = act_cot * activate_slope(pre_act)
    pre_grad = pre_cot.astype(jnp.bfloat16)
    normed_cot = lax.dot_general(
        pre_grad, up_weight, (((1,), (1,)), ((), ())), preferred_element_type=jnp.float32
    )
    scaled_cot = normed_cot * norm_gain
    grad_rows = (
        inv_dev
        * (
            scaled_cot
            - jnp.mean(scaled_cot, axis=-1, keepdims=True)
            - standardized * jnp.mean(scaled_cot * standardized, axis=-1, keepdims=True)
        )
    ).astype(jnp.bfloat16)
    partials = (
        jnp.sum(cot_float * branch, axis=0),
        jnp.sum(branch_cot, axis=0),
        lax.dot_general(
            activated, branch_grad, (((0,), (0,)), ((), ())), preferred_element_type=jnp.float32
        ),
        jnp.sum(pre_cot, axis=0),
        lax.dot_general(
            normed, pre_grad, (((0,), (0,)), ((), ())), preferred_element_type=jnp.float32
        ),
        jnp.sum(normed_cot * standardized, axis=0),
        jnp.sum(normed_cot, axis=0),
    )
    return (block_rows, grad_rows, partials)


def to_columns(band):
    count = lax.axis_size("rows")
    tiles, rows, width, chans = band.shape
    split = band.reshape(tiles, rows, count, width // count, chans).transpose(2, 0, 1, 3, 4)
    split = lax.all_to_all(split, "rows", 0, 0, tiled=True)
    return split.transpose(1, 0, 2, 3, 4).reshape(tiles, count * rows, width // count, chans)


def per_device(
    images,
    cotangent,
    row_taps,
    col_taps,
    norm_gain,
    norm_shift,
    up_weight,
    up_bias,
    down_weight,
    down_bias,
    layer_scale,
):
    tiles_here, band_rows, columns, channels = images.shape
    taps_count = row_taps.shape[0]
    half_reach = (taps_count - 1) // 2
    pixel_scale = 1.0 / math.sqrt(
        tiles_here * lax.axis_size("rep") * band_rows * lax.axis_size("rows") * columns
    )
    bands = 2 if band_rows % 2 == 0 else 1
    band_step = band_rows // bands
    band_pieces = []
    for band in range(bands):
        image_padded = pad_along(
            images[:, band * band_step : (band + 1) * band_step].astype(jnp.float32), 2, half_reach
        )
        row_mix = slide_padded(image_padded, row_taps, 2, columns).astype(jnp.bfloat16)
        row_mix = lax.optimization_barrier(row_mix)
        band_pieces.append(to_columns(row_mix))
    mix_columns = jnp.stack(
        [
            piece.reshape(tiles_here, lax.axis_size("rows"), band_step, piece.shape[2], channels)
            for piece in band_pieces
        ],
        axis=2,
    ).reshape(
        tiles_here, band_rows * lax.axis_size("rows"), columns // lax.axis_size("rows"), channels
    )
    mix_padded = pad_along(mix_columns.astype(jnp.float32), 1, half_reach)
    strip = mix_columns.shape[2]
    parts = 2 if strip % 16 == 0 else 1
    step = strip // parts
    pieces = []
    for part in range(parts):
        local = slide_padded(
            mix_padded[:, :, part * step : (part + 1) * step], col_taps, 1, mix_columns.shape[1]
        ).astype(jnp.bfloat16)
        pieces.append(lax.all_to_all(local, "rows", split_axis=1, concat_axis=2, tiled=True))
    count = lax.axis_size("rows")
    col_mix = jnp.stack(
        [piece.reshape(tiles_here, band_rows, count, step, channels) for piece in pieces], axis=3
    ).reshape(images.shape)
    col_mix = lax.optimization_barrier(col_mix)
    block_rows, grad_rows, partials = pointwise(
        col_mix.reshape(-1, channels),
        images.reshape(-1, channels),
        cotangent.reshape(-1, channels),
        norm_gain,
        norm_shift,
        up_weight,
        up_bias,
        down_weight,
        down_bias,
        layer_scale,
    )
    scale_part, down_bias_part, down_part, up_bias_part, up_part, gain_part, shift_part = partials
    block_out = block_rows.reshape(images.shape)
    grad_rows = lax.optimization_barrier(grad_rows)
    col_grad = grad_rows.reshape(images.shape)
    grad_columns = to_columns(col_grad)
    grad_float = grad_columns.astype(jnp.float32)
    col_part = tap_sums(grad_float, mix_padded, taps_count, 1)
    row_local = slide_padded(
        pad_along(grad_float, 1, half_reach), col_taps[::-1], 1, grad_columns.shape[1]
    ).astype(jnp.bfloat16)
    row_grad = lax.all_to_all(row_local, "rows", split_axis=1, concat_axis=2, tiled=True)
    row_grad = lax.optimization_barrier(row_grad)
    row_part = tap_sums(row_grad, pad_along(images, 2, half_reach), taps_count, 2)
    row_part, row_grad = lax.optimization_barrier((row_part, row_grad))
    image_grad = (
        cotangent.astype(jnp.float32)
        + slide_padded(pad_along(row_grad, 2, half_reach), row_taps[::-1], 2, columns)
    ).astype(jnp.bfloat16)
    down_total, up_total = lax.optimization_barrier(
        lax.psum((down_part * pixel_scale, up_part * pixel_scale), ("rows", "rep"))
    )
    small = (row_part, col_part, scale_part, down_bias_part, up_bias_part, gain_part, shift_part)
    (
        row_total,
        col_total,
        scale_total,
        down_bias_total,
        up_bias_total,
        gain_total,
        shift_total,
    ), image_grad = exchange_sum(
        tuple((part * pixel_scale for part in small)), ("rows", "rep"), image_grad
    )
    return (
        block_out,
        image_grad,
        row_total,
        col_total,
        scale_total,
        down_bias_total,
        down_total,
        up_bias_total,
        up_total,
        gain_total,
        shift_total,
    )


def exchange_sum(parts, axes, companion):
    count = 1
    for axis in axes:
        count *= lax.axis_size(axis)
    stacked = jnp.concatenate([part.reshape(-1, 128) for part in parts])
    piece = -(-stacked.shape[0] // count)
    stacked = jnp.pad(stacked, ((0, piece * count - stacked.shape[0]), (0, 0)))
    spread = lax.all_to_all(stacked.reshape(count, piece, 128), axes, 0, 0, tiled=True)
    mine = jnp.sum(spread, axis=0, keepdims=True)
    mine, companion = lax.optimization_barrier((mine, companion))
    whole = lax.all_to_all(jnp.broadcast_to(mine, (count, piece, 128)), axes, 0, 0, tiled=True)
    return (split_like(whole.reshape(-1), parts), companion)


def split_like(flat, parts):
    out = []
    at = 0
    for part in parts:
        out.append(flat[at : at + part.size].reshape(part.shape))
        at += part.size
    return tuple(out)


def solution(mesh):
    placed = (
        P(("groups", "rep"), "rows", None, None),
        P(("groups", "rep"), "rows", None, None),
        P("groups", None),
        P("groups", None),
        P("groups"),
        P("groups"),
        P("groups", None),
        P("groups"),
        P("groups", None),
        P("groups"),
        P("groups"),
    )
    return jax.shard_map(
        per_device,
        mesh=mesh,
        in_specs=placed,
        out_specs=(
            P(("groups", "rep"), "rows", None, None),
            P(("groups", "rep"), "rows", None, None),
            P("groups", None),
            P("groups", None),
            P("groups"),
            P("groups"),
            P("groups", None),
            P("groups"),
            P("groups", None),
            P("groups"),
            P("groups"),
        ),
        check_vma=False,
    )
```

profile of v0, /device:TPU:0, one launch (start us, length us, event | category | flops | bytes accessed | tf_op | source)
XLA Modules:
  0.0 237.0 jit_solution(5064997916751183123)
XLA Ops:
  11.6 8.1 %fusion.366 = bf16[1,8,128,256]{3,2,1,0:T(8,128)(2,1)S(1)} fusion(f32[1,8,128,256]{3,2,1,0:T(8,128)S(1)} %get-tuple-element.133, f32[256]{0:T(256)S(1)} %bitcast.469, f32[256]{0:T(256)S(1)} %bitcast.472, f32[256]{0:T(256)S(1)} %bitcast.382, f32[256]{0:T(256)S(1)} %bitcast.385, f32[256]{0:T(256)S(1)} %bitcast.388, f32[256]{0:T(256)S(1)} %bitcast.391, ...), kind=kLoop, calls=%fused_computation.834 | loop fusion | flops 26738688 | bytes 1625088 | tf_op jit(solution)/shard_map/convert_element_type | solution.py:151
  20.5 4.4 %all-to-all-start = ((bf16[4,1,8,32,256]{4,3,2,1,0:T(8,128)(2,1)}), bf16[4,1,8,32,256]{4,3,2,1,0:T(8,128)(2,1)S(1)}, u32[]{:S(2)}, u32[]{:S(2)}) async-start(bf16[4,1,8,32,256]{4,3,2,1,0:T(8,128)(2,1)} %copy.28), calls=%async_computation | async-start | bytes 1048576 | tf_op jit(solution)/shard_map/all_to_all | solution.py:121
  24.9 7.9 %fusion.467 = bf16[1,8,128,256]{3,2,1,0:T(8,128)(2,1)S(1)} fusion(f32[1,8,128,256]{3,2,1,0:T(8,128)S(1)} %get-tuple-element.134, f32[256]{0:T(256)S(1)} %bitcast.470, f32[256]{0:T(256)S(1)} %bitcast.473, f32[256]{0:T(256)S(1)} %bitcast.383, f32[256]{0:T(256)S(1)} %bitcast.386, f32[256]{0:T(256)S(1)} %bitcast.389, f32[256]{0:T(256)S(1)} %bitcast.392, ...), kind=kLoop, calls=%fused_computation.935 | loop fusion | flops 26738688 | bytes 1625088 | tf_op jit(solution)/shard_map/convert_element_type | solution.py:151
  37.9 8.2 %all-to-all-done.1 = bf16[4,1,8,32,256]{4,3,2,1,0:T(8,128)(2,1)S(1)} async-done(((bf16[4,1,8,32,256]{4,3,2,1,0:T(8,128)(2,1)}), bf16[4,1,8,32,256]{4,3,2,1,0:T(8,128)(2,1)S(1)}, u32[]{:S(2)}, u32[]{:S(2)}) %all-to-all-start.1) | async-done | bytes 524320 | tf_op jit(solution)/shard_map/all_to_all | solution.py:121
  48.1 9.0 %fusion.676 = bf16[1,64,16,256]{3,2,0,1:T(8,128)(2,1)} fusion(f32[1,64,32,256]{3,2,1,0:T(8,128)S(1)} %bitcast.296, f32[256]{0:T(256)S(1)} %bitcast.623, f32[256]{0:T(256)S(1)} %bitcast.626, f32[256]{0:T(256)S(1)} %bitcast.478, f32[256]{0:T(256)S(1)} %bitcast.481, f32[256]{0:T(256)S(1)} %bitcast.484, f32[256]{0:T(256)S(1)} %bitcast.487, ...), kind=kLoop, calls=%fused_computation.1152 | loop fusion | flops 26738688 | bytes 3722240 | tf_op jit(solution)/shard_map/convert_element_type | solution.py:171
  60.7 9.7 %fusion.677 = bf16[1,64,16,256]{3,2,0,1:T(8,128)(2,1)} fusion(f32[1,64,32,256]{3,2,1,0:T(8,128)S(1)} %bitcast.297, f32[256]{0:T(256)} %bitcast.622, f32[256]{0:T(256)} %bitcast.625, f32[256]{0:T(256)S(1)} %bitcast.479, f32[256]{0:T(256)S(1)} %bitcast.482, f32[256]{0:T(256)S(1)} %bitcast.485, f32[256]{0:T(256)S(1)} %bitcast.488, f32[256]{0:T(256)S(1)} %bitcast.491, ...), kind=kLoop, calls=%fused_computation.1153 | loop fusion | flops 26738688 | bytes 3722240 | tf_op jit(solution)/shard_map/convert_element_type | solution.py:171
  70.4 4.3 %all-to-all-start.3 = ((bf16[1,64,16,256]{3,2,0,1:T(8,128)(2,1)}), bf16[1,64,16,256]{3,2,0,1:T(8,128)(2,1)}, u32[]{:S(2)}, u32[]{:S(2)}) async-start(bf16[1,64,16,256]{3,2,0,1:T(8,128)(2,1)} %fusion.677), calls=%async_computation.3 | async-start | bytes 1048576 | tf_op jit(solution)/shard_map/all_to_all | solution.py:172
  76.8 6.7 %all-to-all-done.3 = bf16[1,64,16,256]{3,2,0,1:T(8,128)(2,1)} async-done(((bf16[1,64,16,256]{3,2,0,1:T(8,128)(2,1)}), bf16[1,64,16,256]{3,2,0,1:T(8,128)(2,1)}, u32[]{:S(2)}, u32[]{:S(2)}) %all-to-all-start.3) | async-done | bytes 524320 | tf_op jit(solution)/shard_map/all_to_all | solution.py:172
  95.3 6.4 %fusion.687 = (f32[1024]{0:T(1024)S(1)}, bf16[2048,1024]{1,0:T(8,128)(2,1)S(1)}) fusion(f32[2048,1024]{1,0:T(8,128)S(1)} %get-tuple-element.246, f32[1024]{0:T(1024)S(1)} %copy-done.19, bf16[2048,256]{1,0:T(8,128)(2,1)S(1)} %get-tuple-element.132, bf16[1024,256]{1,0:T(8,128)(2,1)S(1)} %copy-done.18), kind=kOutput, calls=%fused_computation.1174 | convolution fusion | flops 1117780992 | bytes 14163968 | tf_op jit(solution)/shard_map/dot_general | solution.py:84
  106.0 4.3 %all-to-all-start.4 = ((bf16[4,1,16,32,256]{4,3,2,1,0:T(8,128)(2,1)}), bf16[4,1,16,32,256]{4,3,2,1,0:T(8,128)(2,1)}, u32[]{:S(2)}, u32[]{:S(2)}) async-start(bf16[4,1,16,32,256]{4,3,2,1,0:T(8,128)(2,1)} %bitcast.316), calls=%async_computation.4 | async-start | bytes 2097152 | tf_op jit(solution)/shard_map/all_to_all | solution.py:121
  110.5 4.8 %fusion.268 = f32[256,1024]{1,0:T(8,128)} fusion(bf16[2048,256]{1,0:T(8,128)(2,1)} %copy-done.7, bf16[2048,1024]{1,0:T(8,128)(2,1)} %copy-done.21), kind=kOutput, calls=%fused_computation.736 | convolution fusion | flops 1074003968 | bytes 6291456 | tf_op jit(solution)/shard_map/dot_general | solution.py:108
  116.0 8.8 %all-to-all-done.4 = bf16[4,1,16,32,256]{4,3,2,1,0:T(8,128)(2,1)} async-done(((bf16[4,1,16,32,256]{4,3,2,1,0:T(8,128)(2,1)}), bf16[4,1,16,32,256]{4,3,2,1,0:T(8,128)(2,1)}, u32[]{:S(2)}, u32[]{:S(2)}) %all-to-all-start.4) | async-done | bytes 1048608 | tf_op jit(solution)/shard_map/all_to_all | solution.py:121
  126.2 17.4 %fusion.675 = bf16[1,64,32,256]{3,2,0,1:T(8,128)(2,1)} fusion(f32[1,64,32,256]{3,2,1,0:T(8,128)S(1)} %bitcast.302, f32[256]{0:T(256)S(1)} %bitcast.477, f32[256]{0:T(256)S(1)} %bitcast.534, f32[256]{0:T(256)S(1)} %bitcast.591, f32[256]{0:T(256)S(1)} %bitcast.621, f32[256]{0:T(256)S(1)} %bitcast.618, f32[256]{0:T(256)S(1)} %bitcast.615, ...), kind=kLoop, calls=%fused_computation.1149 | loop fusion | flops 53477376 | bytes 3197952 | tf_op jit(solution)/shard_map/convert_element_type | solution.py:199
  143.6 4.1 %fusion.257 = (f32[256]{0:T(256)S(1)}, f32[256]{0:T(256)S(1)}, f32[256]{0:T(256)S(1)}, f32[256]{0:T(256)S(1)}, f32[256]{0:T(256)S(1)}, /*index=5*/f32[256]{0:T(2...) fusion(f32[1,64,32,256]{3,2,1,0:T(8,128)S(1)} %bitcast.303, ...), kind=kLoop, calls=%fused_computation.712 | loop fusion | flops 18869760 | bytes 4212736 | tf_op jit(solution)/shard_map/reduce_sum | solution.py:48
  147.8 4.9 %fusion.221 = (f32[256]{0:T(256)S(1)}, f32[256]{0:T(256)S(1)}, f32[256]{0:T(256)S(1)}, f32[256]{0:T(256)S(1)}, f32[256]{0:T(256)S(1)}, /*index=5*/f32[256]{0:T(2...) fusion(f32[1,64,32,256]{3,2,1,0:T(8,128)S(1)} %bitcast.304, ...), kind=kLoop, calls=%fused_computation.676 | loop fusion | flops 18869760 | bytes 4212736 | tf_op jit(solution)/shard_map/reduce_sum | solution.py:48
  152.6 4.5 %all-to-all-start.5 = ((bf16[1,64,32,256]{3,2,0,1:T(8,128)(2,1)}), bf16[1,64,32,256]{3,2,0,1:T(8,128)(2,1)}, u32[]{:S(2)}, u32[]{:S(2)}) async-start(bf16[1,64,32,256]{3,2,0,1:T(8,128)(2,1)} %fusion.675), calls=%async_computation.5 | async-start | bytes 2097152 | tf_op jit(solution)/shard_map/all_to_all | solution.py:200
  157.2 9.8 %fusion.185 = (f32[256]{0:T(256)S(1)}, f32[256]{0:T(256)S(1)}, f32[256]{0:T(256)S(1)}, f32[256]{0:T(256)S(1)}, f32[256]{0:T(256)S(1)}, /*index=5*/f32[256]{0:T(2...) fusion(f32[1,64,32,256]{3,2,1,0:T(8,128)} %bitcast.305, ...), kind=kLoop, calls=%fused_computation.640 | loop fusion | flops 14676480 | bytes 4208640 | tf_op jit(solution)/shard_map/reduce_sum | solution.py:48
  172.8 4.8 %fusion.56 = (f32[256]{0:T(256)S(1)}, f32[256]{0:T(256)S(1)}, f32[256]{0:T(256)S(1)}, f32[256]{0:T(256)S(1)}, f32[256]{0:T(256)S(1)}, /*index=5*/f32[256]{0:T(25...) fusion(bf16[1,16,128,256]{3,2,1,0:T(8,128)(2,1)S(1)} %bitcast.3, ...), kind=kLoop, calls=%fused_computation.511 | loop fusion | flops 28831232 | bytes 2115584 | tf_op jit(solution)/shard_map/reduce_sum | solution.py:48
  177.6 5.1 %fusion.55 = (f32[256]{0:T(256)S(1)}, f32[256]{0:T(256)S(1)}, f32[256]{0:T(256)S(1)}, f32[256]{0:T(256)S(1)}, f32[256]{0:T(256)S(1)}, /*index=5*/f32[256]{0:T(25...) fusion(bf16[1,16,128,256]{3,2,1,0:T(8,128)(2,1)S(1)} %bitcast.3, ...), kind=kLoop, calls=%fused_computation.510 | loop fusion | flops 28831232 | bytes 2115584 | tf_op jit(solution)/shard_map/reduce_sum | solution.py:48
  182.7 4.2 %fusion.54 = (f32[256]{0:T(256)S(1)}, f32[256]{0:T(256)S(1)}, f32[256]{0:T(256)S(1)}, f32[256]{0:T(256)S(1)}, f32[256]{0:T(256)S(1)}, /*index=5*/f32[256]{0:T(25...) fusion(bf16[1,16,128,256]{3,2,1,0:T(8,128)(2,1)S(1)} %bitcast.3, ...), kind=kLoop, calls=%fused_computation.509 | loop fusion | flops 24113408 | bytes 2112512 | tf_op jit(solution)/shard_map/reduce_sum | solution.py:48
  188.0 6.5 %all-to-all-start.6 = ((f32[16,14,128]{2,1,0:T(8,128)}), f32[16,14,128]{2,1,0:T(8,128)S(1)}, u32[]{:S(2)}, u32[]{:S(2)}) async-start(f32[16,14,128]{2,1,0:T(8,128)} %reshape.804), calls=%async_computation.6 | async-start | bytes 262144 | tf_op jit(solution)/shard_map/all_to_all | solution.py:245
  194.5 16.5 %fusion.259 = bf16[1,16,128,256]{3,2,1,0:T(8,128)(2,1)} fusion(bf16[1,16,128,256]{3,2,1,0:T(8,128)(2,1)S(1)} %copy-done.5, bf16[1,16,128,256]{3,2,1,0:T(8,128)(2,1)S(1)} %bitcast.309, f32[256]{0:T(256)S(1)} %bitcast.381, f32[256]{0:T(256)S(1)} %bitcast.324, f32[256]{0:T(256)S(1)} %bitcast.438, f32[256]{0:T(256)S(1)} %bitcast.468, f32[256]{0:T(256)S(1)} %bitcast.465, ...), kind=kLoop, calls=%fused_computation.718 | loop fusion | flops 81264640 | bytes 3197952 | tf_op jit(solution)/shard_map/convert_element_type | solution.py:207
  211.7 6.0 %all-to-all-start.7 = ((f32[16,14,128]{2,1,0:T(8,128)}), f32[16,14,128]{2,1,0:T(8,128)S(1)}, u32[]{:S(2)}, u32[]{:S(2)}) async-start(f32[16,14,128]{2,1,0:T(8,128)} %broadcast_in_dim.8), calls=%async_computation.7 | async-start | bytes 262144 | tf_op jit(solution)/shard_map/all_to_all | solution.py:248
  217.7 7.3 %all-to-all-done.7 = f32[16,14,128]{2,1,0:T(8,128)S(1)} async-done(((f32[16,14,128]{2,1,0:T(8,128)}), f32[16,14,128]{2,1,0:T(8,128)S(1)}, u32[]{:S(2)}, u32[]{:S(2)}) %all-to-all-start.7) | async-done | bytes 114720 | tf_op jit(solution)/shard_map/all_to_all | solution.py:248
  (102 shorter events, 48.8 us)
Async XLA Ops:
  7.2 79.3 %copy-start = (bf16[256,1024]{1,0:T(8,128)(2,1)S(1)}, bf16[256,1024]{1,0:T(8,128)(2,1)}, u32[]{:S(2)}) copy-start(bf16[256,1024]{1,0:T(8,128)(2,1)} %param.17) | copy-start | bytes 1572868
  20.5 13.2 %copy-start.9 = (f32[51,256]{1,0:T(8,128)S(1)}, f32[51,256]{1,0:T(8,128)}, u32[]{:S(2)}) copy-start(f32[51,256]{1,0:T(8,128)} %param.14) | copy-start | bytes 156676
  20.5 13.2 %all-to-all-start = ((bf16[4,1,8,32,256]{4,3,2,1,0:T(8,128)(2,1)}), bf16[4,1,8,32,256]{4,3,2,1,0:T(8,128)(2,1)S(1)}, u32[]{:S(2)}, u32[]{:S(2)}) async-start(bf16[4,1,8,32,256]{4,3,2,1,0:T(8,128)(2,1)} %copy.28), calls=%async_computation | async-start | bytes 1048576 | tf_op jit(solution)/shard_map/all_to_all | solution.py:121
  33.7 12.4 %all-to-all-start.1 = ((bf16[4,1,8,32,256]{4,3,2,1,0:T(8,128)(2,1)}), bf16[4,1,8,32,256]{4,3,2,1,0:T(8,128)(2,1)S(1)}, u32[]{:S(2)}, u32[]{:S(2)}) async-start(bf16[4,1,8,32,256]{4,3,2,1,0:T(8,128)(2,1)} %copy.29), calls=%async_computation.1 | async-start | bytes 1048576 | tf_op jit(solution)/shard_map/all_to_all | solution.py:121
  46.1 2.0 copy-start.12
  57.2 13.2 %all-to-all-start.2 = ((bf16[1,64,16,256]{3,2,0,1:T(8,128)(2,1)}), bf16[1,64,16,256]{3,2,0,1:T(8,128)(2,1)S(1)}, u32[]{:S(2)}, u32[]{:S(2)}) async-start(bf16[1,64,16,256]{3,2,0,1:T(8,128)(2,1)} %fusion.676), calls=%async_computation.2 | async-start | bytes 1048576 | tf_op jit(solution)/shard_map/all_to_all | solution.py:172
  70.4 13.1 %all-to-all-start.3 = ((bf16[1,64,16,256]{3,2,0,1:T(8,128)(2,1)}), bf16[1,64,16,256]{3,2,0,1:T(8,128)(2,1)}, u32[]{:S(2)}, u32[]{:S(2)}) async-start(bf16[1,64,16,256]{3,2,0,1:T(8,128)(2,1)} %fusion.677), calls=%async_computation.3 | async-start | bytes 1048576 | tf_op jit(solution)/shard_map/all_to_all | solution.py:172
  86.5 3.8 %copy-start.7 = (bf16[2048,256]{1,0:T(8,128)(2,1)}, bf16[2048,256]{1,0:T(8,128)(2,1)S(1)}, u32[]{:S(2)}) copy-start(bf16[2048,256]{1,0:T(8,128)(2,1)S(1)} %add_convert_fusion) | copy-start | bytes 3145732
  86.5 3.8 %copy-start.2 = (bf16[1,16,128,256]{3,2,1,0:T(8,128)(2,1)S(1)}, bf16[1,16,128,256]{3,2,1,0:T(8,128)(2,1)}, u32[]{:S(2)}) copy-start(bf16[1,16,128,256]{3,2,1,0:T(8,128)(2,1)} %param.11) | copy-start | bytes 3145732
  86.6 3.8 %copy-start.4 = (bf16[1,16,128,256]{3,2,1,0:T(8,128)(2,1)S(1)}, bf16[1,16,128,256]{3,2,1,0:T(8,128)(2,1)}, u32[]{:S(2)}) copy-start(bf16[1,16,128,256]{3,2,1,0:T(8,128)(2,1)} %param.12) | copy-start | bytes 3145732
  86.6 3.8 %copy-start.17 = (f32[256]{0:T(256)S(1)}, f32[256]{0:T(256)}, u32[]{:S(2)}) copy-start(f32[256]{0:T(256)} %param.21) | copy-start | bytes 3076
  86.6 3.8 %copy-start.18 = (bf16[1024,256]{1,0:T(8,128)(2,1)S(1)}, bf16[1024,256]{1,0:T(8,128)(2,1)}, u32[]{:S(2)}) copy-start(bf16[1024,256]{1,0:T(8,128)(2,1)} %param.19) | copy-start | bytes 1572868
  86.6 3.8 %copy-start.20 = (f32[256]{0:T(256)S(1)}, f32[256]{0:T(256)}, u32[]{:S(2)}) copy-start(f32[256]{0:T(256)} %param.20) | copy-start | bytes 3076
  106.0 18.8 %all-to-all-start.4 = ((bf16[4,1,16,32,256]{4,3,2,1,0:T(8,128)(2,1)}), bf16[4,1,16,32,256]{4,3,2,1,0:T(8,128)(2,1)}, u32[]{:S(2)}, u32[]{:S(2)}) async-start(bf16[4,1,16,32,256]{4,3,2,1,0:T(8,128)(2,1)} %bitcast.316), calls=%async_computation.4 | async-start | bytes 2097152 | tf_op jit(solution)/shard_map/all_to_all | solution.py:121
  110.2 107.5 %all-reduce.10.cloned.1.call-start = ((), (), s32[]{:S(2)}) async-start(), calls=%async_computation.8 | async-start | bytes 4194304 | tf_op jit(solution)/shard_map/psum | solution.py:209
  115.3 10.9 %copy-start.11 = (f32[1,256]{1,0:T(1,128)S(1)}, f32[1,256]{1,0:T(1,128)}, u32[]{:S(2)}) copy-start(f32[1,256]{1,0:T(1,128)} %get-tuple-element.190) | copy-start | bytes 3076
  115.3 10.9 %copy-start.13 = (f32[1,256]{1,0:T(1,128)S(1)}, f32[1,256]{1,0:T(1,128)}, u32[]{:S(2)}) copy-start(f32[1,256]{1,0:T(1,128)} %get-tuple-element.191) | copy-start | bytes 3076
  126.2 21.6 %copy-start.1 = (f32[4,1,16,32,256]{4,3,2,0,1:T(8,128)}, f32[4,1,16,32,256]{4,3,2,0,1:T(8,128)S(1)}, u32[]{:S(2)}) copy-start(f32[4,1,16,32,256]{4,3,2,0,1:T(8,128)S(1)} %bitcast_convert_fusion) | copy-start | bytes 6291460
  152.6 18.8 %all-to-all-start.5 = ((bf16[1,64,32,256]{3,2,0,1:T(8,128)(2,1)}), bf16[1,64,32,256]{3,2,0,1:T(8,128)(2,1)}, u32[]{:S(2)}, u32[]{:S(2)}) async-start(bf16[1,64,32,256]{3,2,0,1:T(8,128)(2,1)} %fusion.675), calls=%async_computation.5 | async-start | bytes 2097152 | tf_op jit(solution)/shard_map/all_to_all | solution.py:200
  168.5 4.3 %copy-start.3 = (bf16[1,16,128,256]{3,2,1,0:T(8,128)(2,1)S(1)}, bf16[1,16,128,256]{3,2,1,0:T(8,128)(2,1)}, u32[]{:S(2)}) copy-start(bf16[1,16,128,256]{3,2,1,0:T(8,128)(2,1)} %param.11) | copy-start | bytes 3145732
  186.9 7.7 %copy-start.5 = (bf16[1,16,128,256]{3,2,1,0:T(8,128)(2,1)S(1)}, bf16[1,16,128,256]{3,2,1,0:T(8,128)(2,1)}, u32[]{:S(2)}) copy-start(bf16[1,16,128,256]{3,2,1,0:T(8,128)(2,1)} %param.12) | copy-start | bytes 3145732
  188.0 23.0 %all-to-all-start.6 = ((f32[16,14,128]{2,1,0:T(8,128)}), f32[16,14,128]{2,1,0:T(8,128)S(1)}, u32[]{:S(2)}, u32[]{:S(2)}) async-start(f32[16,14,128]{2,1,0:T(8,128)} %reshape.804), calls=%async_computation.6 | async-start | bytes 262144 | tf_op jit(solution)/shard_map/all_to_all | solution.py:245
  211.7 13.4 %all-to-all-start.7 = ((f32[16,14,128]{2,1,0:T(8,128)}), f32[16,14,128]{2,1,0:T(8,128)S(1)}, u32[]{:S(2)}, u32[]{:S(2)}) async-start(f32[16,14,128]{2,1,0:T(8,128)} %broadcast_in_dim.8), calls=%async_computation.7 | async-start | bytes 262144 | tf_op jit(solution)/shard_map/all_to_all | solution.py:248
  217.7 11.5 %copy-start.8 = (f32[256,1024]{1,0:T(8,128)S(1)}, f32[256,1024]{1,0:T(8,128)}, u32[]{:S(2)}) copy-start(f32[256,1024]{1,0:T(8,128)} %get-tuple-element.266) | copy-start | bytes 3145732
  (7 other events, 9.5 us)
Sparse Core Ops, SparseCore 0:
  115.4 102.0 all-reduce.9
where the time goes:
time: 238 us; the launch traced here: 237 us
  other arithmetic  113 us (47%)
  starting transfers between devices  37.3 us (16%)
  waiting for transfers between devices  33.7 us (14%)
  matrix products  21.7 us (9%)
  local copies, waits for them, and re-layouts  16.3 us (7%)
  between operations  14.6 us (6%)
    reduce_sum x7, other arithmetic, tap_sums(): jnp.sum(cot_field.astype(jnp.float32) * lax.slice_in_dim(padded, offset,...  34.4 us
    convert_element_type x2, other arithmetic, per_device(): local = slide_padded(mix_padded[:, :, part * step:(part + 1) * step], col...  18.8 us
    convert_element_type x1, other arithmetic, per_device(): row_local = slide_padded(pad_along(grad_float, 1, half_reach), col_taps[:...  17.4 us
    all_to_all x3, waiting for transfers between devices, to_columns(): split = lax.all_to_all(split, 'rows', 0, 0, tiled=True)  17 us
    convert_element_type x1, other arithmetic, per_device(): image_grad = (cotangent.astype(jnp.float32) + slide_padded(pad_along(row_...  16.5 us
    convert_element_type x2, other arithmetic, per_device(): slide_padded(image_padded, row_taps, 2, columns).astype(jnp.bfloat16)  16 us
    all_to_all x3, starting transfers between devices, to_columns(): split = lax.all_to_all(split, 'rows', 0, 0, tiled=True)  12.2 us
    all_to_all x2, starting transfers between devices, per_device(): lax.all_to_all(local, 'rows', split_axis=1, concat_axis=2, tiled=True)  7.78 us
  transfers between devices with their start and end apart: 9, of which 5 were waited for; matrix products, arithmetic and copies ran while one was open for 42% of the time, Pallas kernels for 0%

commit v1 on v0

--- a/solution.py
+++ b/solution.py
@@ -169,7 +169,14 @@
         local = slide_padded(
             mix_padded[:, :, part * step : (part + 1) * step], col_taps, 1, mix_columns.shape[1]
         ).astype(jnp.bfloat16)
-        pieces.append(lax.all_to_all(local, "rows", split_axis=1, concat_axis=2, tiled=True))
+        pieces.append(
+            jnp.concatenate(
+                lax.all_to_all(
+                    jnp.stack(jnp.split(local, lax.axis_size("rows"), axis=1)), "rows", 0, 0
+                ),
+                axis=2,
+            )
+        )
     count = lax.axis_size("rows")
     col_mix = jnp.stack(
         [piece.reshape(tiles_here, band_rows, count, step, channels) for piece in pieces], axis=3

time: 238 us -> 239 us (level)
  no operation moved by 1% of the time
where the time goes in v1:
time: 239 us; the launch traced here: 238 us
  other arithmetic  114 us (48%)
  starting transfers between devices  37.4 us (16%)
  waiting for transfers between devices  33.7 us (14%)
  matrix products  21.5 us (9%)
  local copies, waits for them, and re-layouts  16.5 us (7%)
  between operations  14.6 us (6%)
    reduce_sum x7, other arithmetic, tap_sums(): jnp.sum(cot_field.astype(jnp.float32) * lax.slice_in_dim(padded, offset,...  34.4 us
    convert_element_type x2, other arithmetic, per_device(): local = slide_padded(mix_padded[:, :, part * step:(part + 1) * step], col...  17.5 us
    convert_element_type x1, other arithmetic, per_device(): row_local = slide_padded(pad_along(grad_float, 1, half_reach), col_taps[:...  17.4 us
    all_to_all x3, waiting for transfers between devices, to_columns(): split = lax.all_to_all(split, 'rows', 0, 0, tiled=True)  17 us
    convert_element_type x1, other arithmetic, per_device(): image_grad = (cotangent.astype(jnp.float32) + slide_padded(pad_along(row_...  16.5 us
    convert_element_type x2, other arithmetic, per_device(): slide_padded(image_padded, row_taps, 2, columns).astype(jnp.bfloat16)  16 us
    all_to_all x3, starting transfers between devices, to_columns(): split = lax.all_to_all(split, 'rows', 0, 0, tiled=True)  12.2 us
    all_to_all x2, starting transfers between devices, per_device(): lax.all_to_all(jnp.stack(jnp.split(local, lax.axis_size('rows'), axis=1))...  7.78 us
  transfers between devices with their start and end apart: 9, of which 5 were waited for; matrix products, arithmetic and copies ran while one was open for 42% of the time, Pallas kernels for 0%

profile of v1, /device:TPU:0, one launch (start us, length us, event | category | flops | bytes accessed | tf_op | source)
XLA Modules:
  0.0 237.5 jit_solution(13799457777041026401)
XLA Ops:
  11.6 8.1 %fusion.366 = bf16[1,8,128,256]{3,2,1,0:T(8,128)(2,1)S(1)} fusion(f32[1,8,128,256]{3,2,1,0:T(8,128)S(1)} %get-tuple-element.133, f32[256]{0:T(256)S(1)} %bitcast.479, f32[256]{0:T(256)S(1)} %bitcast.482, f32[256]{0:T(256)S(1)} %bitcast.392, f32[256]{0:T(256)S(1)} %bitcast.395, f32[256]{0:T(256)S(1)} %bitcast.398, f32[256]{0:T(256)S(1)} %bitcast.401, ...), kind=kLoop, calls=%fused_computation.834 | loop fusion | flops 26738688 | bytes 1625088 | tf_op jit(solution)/shard_map/convert_element_type | solution.py:151
  20.5 4.4 %all-to-all-start = ((bf16[4,1,8,32,256]{4,3,2,1,0:T(8,128)(2,1)}), bf16[4,1,8,32,256]{4,3,2,1,0:T(8,128)(2,1)S(1)}, u32[]{:S(2)}, u32[]{:S(2)}) async-start(bf16[4,1,8,32,256]{4,3,2,1,0:T(8,128)(2,1)} %copy.38), calls=%async_computation | async-start | bytes 1048576 | tf_op jit(solution)/shard_map/all_to_all | solution.py:121
  24.9 7.9 %fusion.467 = bf16[1,8,128,256]{3,2,1,0:T(8,128)(2,1)S(1)} fusion(f32[1,8,128,256]{3,2,1,0:T(8,128)S(1)} %get-tuple-element.134, f32[256]{0:T(256)S(1)} %bitcast.480, f32[256]{0:T(256)S(1)} %bitcast.483, f32[256]{0:T(256)S(1)} %bitcast.393, f32[256]{0:T(256)S(1)} %bitcast.396, f32[256]{0:T(256)S(1)} %bitcast.399, f32[256]{0:T(256)S(1)} %bitcast.402, ...), kind=kLoop, calls=%fused_computation.935 | loop fusion | flops 26738688 | bytes 1625088 | tf_op jit(solution)/shard_map/convert_element_type | solution.py:151
  37.9 8.2 %all-to-all-done.1 = bf16[4,1,8,32,256]{4,3,2,1,0:T(8,128)(2,1)S(1)} async-done(((bf16[4,1,8,32,256]{4,3,2,1,0:T(8,128)(2,1)}), bf16[4,1,8,32,256]{4,3,2,1,0:T(8,128)(2,1)S(1)}, u32[]{:S(2)}, u32[]{:S(2)}) %all-to-all-start.1) | async-done | bytes 524320 | tf_op jit(solution)/shard_map/all_to_all | solution.py:121
  48.1 8.4 %fusion.674 = bf16[1,64,16,256]{3,2,1,0:T(8,128)(2,1)S(1)} fusion(f32[1,64,32,256]{3,2,1,0:T(8,128)S(1)} %bitcast.306, f32[256]{0:T(256)S(1)} %bitcast.633, f32[256]{0:T(256)S(1)} %bitcast.636, f32[256]{0:T(256)S(1)} %bitcast.488, f32[256]{0:T(256)S(1)} %bitcast.491, f32[256]{0:T(256)S(1)} %bitcast.494, f32[256]{0:T(256)S(1)} %bitcast.497, ...), kind=kLoop, calls=%fused_computation.1148 | loop fusion | flops 26738688 | bytes 3722240 | tf_op jit(solution)/shard_map/convert_element_type | solution.py:171
  61.0 9.1 %fusion.673 = bf16[1,64,16,256]{3,2,1,0:T(8,128)(2,1)S(1)} fusion(f32[1,64,32,256]{3,2,1,0:T(8,128)S(1)} %bitcast.307, f32[256]{0:T(256)} %bitcast.632, f32[256]{0:T(256)} %bitcast.635, f32[256]{0:T(256)S(1)} %bitcast.489, f32[256]{0:T(256)S(1)} %bitcast.492, f32[256]{0:T(256)S(1)} %bitcast.495, f32[256]{0:T(256)S(1)} %bitcast.498, f32[256]{0:T(256)S(1)} %bitcast.501, ...), kind=kLoop, calls=%fused_computation.1147 | loop fusion | flops 26738688 | bytes 3722240 | tf_op jit(solution)/shard_map/convert_element_type | solution.py:171
  71.0 4.3 %all-to-all-start.3 = ((bf16[4,1,16,16,256]{4,3,2,1,0:T(8,128)(2,1)}), bf16[4,1,16,16,256]{4,3,2,1,0:T(8,128)(2,1)}, u32[]{:S(2)}, u32[]{:S(2)}) async-start(bf16[4,1,16,16,256]{4,3,2,1,0:T(8,128)(2,1)} %pad_maximum_fusion.2), calls=%async_computation.3 | async-start | bytes 1048576 | tf_op jit(solution)/shard_map/all_to_all | solution.py:174
  77.4 6.7 %all-to-all-done.3 = bf16[4,1,16,16,256]{4,3,2,1,0:T(8,128)(2,1)} async-done(((bf16[4,1,16,16,256]{4,3,2,1,0:T(8,128)(2,1)}), bf16[4,1,16,16,256]{4,3,2,1,0:T(8,128)(2,1)}, u32[]{:S(2)}, u32[]{:S(2)}) %all-to-all-start.3) | async-done | bytes 524320 | tf_op jit(solution)/shard_map/all_to_all | solution.py:174
  95.8 6.4 %fusion.685 = (f32[1024]{0:T(1024)S(1)}, bf16[2048,1024]{1,0:T(8,128)(2,1)S(1)}) fusion(f32[2048,1024]{1,0:T(8,128)S(1)} %get-tuple-element.254, f32[1024]{0:T(1024)S(1)} %copy-done.19, bf16[2048,256]{1,0:T(8,128)(2,1)S(1)} %get-tuple-element.132, bf16[1024,256]{1,0:T(8,128)(2,1)S(1)} %copy-done.18), kind=kOutput, calls=%fused_computation.1182 | convolution fusion | flops 1117780992 | bytes 14163968 | tf_op jit(solution)/shard_map/dot_general | solution.py:84
  106.4 4.3 %all-to-all-start.4 = ((bf16[4,1,16,32,256]{4,3,2,1,0:T(8,128)(2,1)}), bf16[4,1,16,32,256]{4,3,2,1,0:T(8,128)(2,1)}, u32[]{:S(2)}, u32[]{:S(2)}) async-start(bf16[4,1,16,32,256]{4,3,2,1,0:T(8,128)(2,1)} %bitcast.326), calls=%async_computation.4 | async-start | bytes 2097152 | tf_op jit(solution)/shard_map/all_to_all | solution.py:121
  111.0 4.8 %fusion.268 = f32[256,1024]{1,0:T(8,128)} fusion(bf16[2048,256]{1,0:T(8,128)(2,1)} %copy-done.7, bf16[2048,1024]{1,0:T(8,128)(2,1)} %copy-done.21), kind=kOutput, calls=%fused_computation.736 | convolution fusion | flops 1074003968 | bytes 6291456 | tf_op jit(solution)/shard_map/dot_general | solution.py:108
  116.4 8.8 %all-to-all-done.4 = bf16[4,1,16,32,256]{4,3,2,1,0:T(8,128)(2,1)} async-done(((bf16[4,1,16,32,256]{4,3,2,1,0:T(8,128)(2,1)}), bf16[4,1,16,32,256]{4,3,2,1,0:T(8,128)(2,1)}, u32[]{:S(2)}, u32[]{:S(2)}) %all-to-all-start.4) | async-done | bytes 1048608 | tf_op jit(solution)/shard_map/all_to_all | solution.py:121
  126.7 17.4 %fusion.675 = bf16[1,64,32,256]{3,2,0,1:T(8,128)(2,1)} fusion(f32[1,64,32,256]{3,2,1,0:T(8,128)S(1)} %bitcast.312, f32[256]{0:T(256)S(1)} %bitcast.487, f32[256]{0:T(256)S(1)} %bitcast.544, f32[256]{0:T(256)S(1)} %bitcast.601, f32[256]{0:T(256)S(1)} %bitcast.631, f32[256]{0:T(256)S(1)} %bitcast.628, f32[256]{0:T(256)S(1)} %bitcast.625, ...), kind=kLoop, calls=%fused_computation.1149 | loop fusion | flops 53477376 | bytes 3197952 | tf_op jit(solution)/shard_map/convert_element_type | solution.py:206
  144.1 4.1 %fusion.257 = (f32[256]{0:T(256)S(1)}, f32[256]{0:T(256)S(1)}, f32[256]{0:T(256)S(1)}, f32[256]{0:T(256)S(1)}, f32[256]{0:T(256)S(1)}, /*index=5*/f32[256]{0:T(2...) fusion(f32[1,64,32,256]{3,2,1,0:T(8,128)S(1)} %bitcast.313, ...), kind=kLoop, calls=%fused_computation.712 | loop fusion | flops 18869760 | bytes 4212736 | tf_op jit(solution)/shard_map/reduce_sum | solution.py:48
  148.2 4.9 %fusion.221 = (f32[256]{0:T(256)S(1)}, f32[256]{0:T(256)S(1)}, f32[256]{0:T(256)S(1)}, f32[256]{0:T(256)S(1)}, f32[256]{0:T(256)S(1)}, /*index=5*/f32[256]{0:T(2...) fusion(f32[1,64,32,256]{3,2,1,0:T(8,128)S(1)} %bitcast.314, ...), kind=kLoop, calls=%fused_computation.676 | loop fusion | flops 18869760 | bytes 4212736 | tf_op jit(solution)/shard_map/reduce_sum | solution.py:48
  153.1 4.5 %all-to-all-start.5 = ((bf16[1,64,32,256]{3,2,0,1:T(8,128)(2,1)}), bf16[1,64,32,256]{3,2,0,1:T(8,128)(2,1)}, u32[]{:S(2)}, u32[]{:S(2)}) async-start(bf16[1,64,32,256]{3,2,0,1:T(8,128)(2,1)} %fusion.675), calls=%async_computation.5 | async-start | bytes 2097152 | tf_op jit(solution)/shard_map/all_to_all | solution.py:207
  157.6 9.8 %fusion.185 = (f32[256]{0:T(256)S(1)}, f32[256]{0:T(256)S(1)}, f32[256]{0:T(256)S(1)}, f32[256]{0:T(256)S(1)}, f32[256]{0:T(256)S(1)}, /*index=5*/f32[256]{0:T(2...) fusion(f32[1,64,32,256]{3,2,1,0:T(8,128)} %bitcast.315, ...), kind=kLoop, calls=%fused_computation.640 | loop fusion | flops 14676480 | bytes 4208640 | tf_op jit(solution)/shard_map/reduce_sum | solution.py:48
  173.2 4.8 %fusion.56 = (f32[256]{0:T(256)S(1)}, f32[256]{0:T(256)S(1)}, f32[256]{0:T(256)S(1)}, f32[256]{0:T(256)S(1)}, f32[256]{0:T(256)S(1)}, /*index=5*/f32[256]{0:T(25...) fusion(bf16[1,16,128,256]{3,2,1,0:T(8,128)(2,1)S(1)} %bitcast.3, ...), kind=kLoop, calls=%fused_computation.511 | loop fusion | flops 28831232 | bytes 2115584 | tf_op jit(solution)/shard_map/reduce_sum | solution.py:48
  178.0 5.1 %fusion.55 = (f32[256]{0:T(256)S(1)}, f32[256]{0:T(256)S(1)}, f32[256]{0:T(256)S(1)}, f32[256]{0:T(256)S(1)}, f32[256]{0:T(256)S(1)}, /*index=5*/f32[256]{0:T(25...) fusion(bf16[1,16,128,256]{3,2,1,0:T(8,128)(2,1)S(1)} %bitcast.3, ...), kind=kLoop, calls=%fused_computation.510 | loop fusion | flops 28831232 | bytes 2115584 | tf_op jit(solution)/shard_map/reduce_sum | solution.py:48
  183.2 4.2 %fusion.54 = (f32[256]{0:T(256)S(1)}, f32[256]{0:T(256)S(1)}, f32[256]{0:T(256)S(1)}, f32[256]{0:T(256)S(1)}, f32[256]{0:T(256)S(1)}, /*index=5*/f32[256]{0:T(25...) fusion(bf16[1,16,128,256]{3,2,1,0:T(8,128)(2,1)S(1)} %bitcast.3, ...), kind=kLoop, calls=%fused_computation.509 | loop fusion | flops 24113408 | bytes 2112512 | tf_op jit(solution)/shard_map/reduce_sum | solution.py:48
  188.4 6.6 %all-to-all-start.6 = ((f32[16,14,128]{2,1,0:T(8,128)}), f32[16,14,128]{2,1,0:T(8,128)S(1)}, u32[]{:S(2)}, u32[]{:S(2)}) async-start(f32[16,14,128]{2,1,0:T(8,128)} %reshape.810), calls=%async_computation.6 | async-start | bytes 262144 | tf_op jit(solution)/shard_map/all_to_all | solution.py:252
  195.0 16.5 %fusion.259 = bf16[1,16,128,256]{3,2,1,0:T(8,128)(2,1)} fusion(bf16[1,16,128,256]{3,2,1,0:T(8,128)(2,1)S(1)} %copy-done.5, bf16[1,16,128,256]{3,2,1,0:T(8,128)(2,1)S(1)} %bitcast.319, f32[256]{0:T(256)S(1)} %bitcast.391, f32[256]{0:T(256)S(1)} %bitcast.334, f32[256]{0:T(256)S(1)} %bitcast.448, f32[256]{0:T(256)S(1)} %bitcast.478, f32[256]{0:T(256)S(1)} %bitcast.475, ...), kind=kLoop, calls=%fused_computation.718 | loop fusion | flops 81264640 | bytes 3197952 | tf_op jit(solution)/shard_map/convert_element_type | solution.py:214
  212.2 6.0 %all-to-all-start.7 = ((f32[16,14,128]{2,1,0:T(8,128)}), f32[16,14,128]{2,1,0:T(8,128)S(1)}, u32[]{:S(2)}, u32[]{:S(2)}) async-start(f32[16,14,128]{2,1,0:T(8,128)} %broadcast_in_dim.8), calls=%async_computation.7 | async-start | bytes 262144 | tf_op jit(solution)/shard_map/all_to_all | solution.py:255
  218.2 7.3 %all-to-all-done.7 = f32[16,14,128]{2,1,0:T(8,128)S(1)} async-done(((f32[16,14,128]{2,1,0:T(8,128)}), f32[16,14,128]{2,1,0:T(8,128)S(1)}, u32[]{:S(2)}, u32[]{:S(2)}) %all-to-all-start.7) | async-done | bytes 114720 | tf_op jit(solution)/shard_map/all_to_all | solution.py:255
  (106 shorter events, 50.5 us)
Async XLA Ops:
  7.2 79.9 %copy-start = (bf16[256,1024]{1,0:T(8,128)(2,1)S(1)}, bf16[256,1024]{1,0:T(8,128)(2,1)}, u32[]{:S(2)}) copy-start(bf16[256,1024]{1,0:T(8,128)(2,1)} %param.17) | copy-start | bytes 1572868
  20.5 13.2 %copy-start.9 = (f32[51,256]{1,0:T(8,128)S(1)}, f32[51,256]{1,0:T(8,128)}, u32[]{:S(2)}) copy-start(f32[51,256]{1,0:T(8,128)} %param.14) | copy-start | bytes 156676
  20.5 13.2 %all-to-all-start = ((bf16[4,1,8,32,256]{4,3,2,1,0:T(8,128)(2,1)}), bf16[4,1,8,32,256]{4,3,2,1,0:T(8,128)(2,1)S(1)}, u32[]{:S(2)}, u32[]{:S(2)}) async-start(bf16[4,1,8,32,256]{4,3,2,1,0:T(8,128)(2,1)} %copy.38), calls=%async_computation | async-start | bytes 1048576 | tf_op jit(solution)/shard_map/all_to_all | solution.py:121
  33.7 12.4 %all-to-all-start.1 = ((bf16[4,1,8,32,256]{4,3,2,1,0:T(8,128)(2,1)}), bf16[4,1,8,32,256]{4,3,2,1,0:T(8,128)(2,1)S(1)}, u32[]{:S(2)}, u32[]{:S(2)}) async-start(bf16[4,1,8,32,256]{4,3,2,1,0:T(8,128)(2,1)} %copy.39), calls=%async_computation.1 | async-start | bytes 1048576 | tf_op jit(solution)/shard_map/all_to_all | solution.py:121
  46.1 2.0 copy-start.12
  57.5 13.5 %all-to-all-start.2 = ((bf16[4,1,16,16,256]{4,3,2,1,0:T(8,128)(2,1)}), bf16[4,1,16,16,256]{4,3,2,1,0:T(8,128)(2,1)S(1)}, u32[]{:S(2)}, u32[]{:S(2)}) async-start(bf16[4,1,16,16,256]{4,3,2,1,0:T(8,128)(2,1)} %pad_maximum_fusion.1), calls=%async_computation.2 | async-start | bytes 1048576 | tf_op jit(solution)/shard_map/all_to_all | solution.py:174
  71.0 13.1 %all-to-all-start.3 = ((bf16[4,1,16,16,256]{4,3,2,1,0:T(8,128)(2,1)}), bf16[4,1,16,16,256]{4,3,2,1,0:T(8,128)(2,1)}, u32[]{:S(2)}, u32[]{:S(2)}) async-start(bf16[4,1,16,16,256]{4,3,2,1,0:T(8,128)(2,1)} %pad_maximum_fusion.2), calls=%async_computation.3 | async-start | bytes 1048576 | tf_op jit(solution)/shard_map/all_to_all | solution.py:174
  87.1 3.8 %copy-start.7 = (bf16[2048,256]{1,0:T(8,128)(2,1)}, bf16[2048,256]{1,0:T(8,128)(2,1)S(1)}, u32[]{:S(2)}) copy-start(bf16[2048,256]{1,0:T(8,128)(2,1)S(1)} %add_convert_fusion) | copy-start | bytes 3145732
  87.1 3.8 %copy-start.2 = (bf16[1,16,128,256]{3,2,1,0:T(8,128)(2,1)S(1)}, bf16[1,16,128,256]{3,2,1,0:T(8,128)(2,1)}, u32[]{:S(2)}) copy-start(bf16[1,16,128,256]{3,2,1,0:T(8,128)(2,1)} %param.11) | copy-start | bytes 3145732
  87.2 3.8 %copy-start.4 = (bf16[1,16,128,256]{3,2,1,0:T(8,128)(2,1)S(1)}, bf16[1,16,128,256]{3,2,1,0:T(8,128)(2,1)}, u32[]{:S(2)}) copy-start(bf16[1,16,128,256]{3,2,1,0:T(8,128)(2,1)} %param.12) | copy-start | bytes 3145732
  87.2 3.8 %copy-start.17 = (f32[256]{0:T(256)S(1)}, f32[256]{0:T(256)}, u32[]{:S(2)}) copy-start(f32[256]{0:T(256)} %param.21) | copy-start | bytes 3076
  87.2 3.8 %copy-start.18 = (bf16[1024,256]{1,0:T(8,128)(2,1)S(1)}, bf16[1024,256]{1,0:T(8,128)(2,1)}, u32[]{:S(2)}) copy-start(bf16[1024,256]{1,0:T(8,128)(2,1)} %param.19) | copy-start | bytes 1572868
  87.2 3.8 %copy-start.20 = (f32[256]{0:T(256)S(1)}, f32[256]{0:T(256)}, u32[]{:S(2)}) copy-start(f32[256]{0:T(256)} %param.20) | copy-start | bytes 3076
  106.4 18.8 %all-to-all-start.4 = ((bf16[4,1,16,32,256]{4,3,2,1,0:T(8,128)(2,1)}), bf16[4,1,16,32,256]{4,3,2,1,0:T(8,128)(2,1)}, u32[]{:S(2)}, u32[]{:S(2)}) async-start(bf16[4,1,16,32,256]{4,3,2,1,0:T(8,128)(2,1)} %bitcast.326), calls=%async_computation.4 | async-start | bytes 2097152 | tf_op jit(solution)/shard_map/all_to_all | solution.py:121
  110.7 107.5 %all-reduce.10.cloned.1.call-start = ((), (), s32[]{:S(2)}) async-start(), calls=%async_computation.8 | async-start | bytes 4194304 | tf_op jit(solution)/shard_map/psum | solution.py:216
  115.8 10.9 %copy-start.11 = (f32[1,256]{1,0:T(1,128)S(1)}, f32[1,256]{1,0:T(1,128)}, u32[]{:S(2)}) copy-start(f32[1,256]{1,0:T(1,128)} %get-tuple-element.198) | copy-start | bytes 3076
  115.8 10.9 %copy-start.13 = (f32[1,256]{1,0:T(1,128)S(1)}, f32[1,256]{1,0:T(1,128)}, u32[]{:S(2)}) copy-start(f32[1,256]{1,0:T(1,128)} %get-tuple-element.199) | copy-start | bytes 3076
  126.7 21.6 %copy-start.1 = (f32[4,1,16,32,256]{4,3,2,0,1:T(8,128)}, f32[4,1,16,32,256]{4,3,2,0,1:T(8,128)S(1)}, u32[]{:S(2)}) copy-start(f32[4,1,16,32,256]{4,3,2,0,1:T(8,128)S(1)} %bitcast_convert_fusion) | copy-start | bytes 6291460
  153.1 18.8 %all-to-all-start.5 = ((bf16[1,64,32,256]{3,2,0,1:T(8,128)(2,1)}), bf16[1,64,32,256]{3,2,0,1:T(8,128)(2,1)}, u32[]{:S(2)}, u32[]{:S(2)}) async-start(bf16[1,64,32,256]{3,2,0,1:T(8,128)(2,1)} %fusion.675), calls=%async_computation.5 | async-start | bytes 2097152 | tf_op jit(solution)/shard_map/all_to_all | solution.py:207
  169.0 4.3 %copy-start.3 = (bf16[1,16,128,256]{3,2,1,0:T(8,128)(2,1)S(1)}, bf16[1,16,128,256]{3,2,1,0:T(8,128)(2,1)}, u32[]{:S(2)}) copy-start(bf16[1,16,128,256]{3,2,1,0:T(8,128)(2,1)} %param.11) | copy-start | bytes 3145732
  187.3 7.7 %copy-start.5 = (bf16[1,16,128,256]{3,2,1,0:T(8,128)(2,1)S(1)}, bf16[1,16,128,256]{3,2,1,0:T(8,128)(2,1)}, u32[]{:S(2)}) copy-start(bf16[1,16,128,256]{3,2,1,0:T(8,128)(2,1)} %param.12) | copy-start | bytes 3145732
  188.4 23.1 %all-to-all-start.6 = ((f32[16,14,128]{2,1,0:T(8,128)}), f32[16,14,128]{2,1,0:T(8,128)S(1)}, u32[]{:S(2)}, u32[]{:S(2)}) async-start(f32[16,14,128]{2,1,0:T(8,128)} %reshape.810), calls=%async_computation.6 | async-start | bytes 262144 | tf_op jit(solution)/shard_map/all_to_all | solution.py:252
  212.2 13.4 %all-to-all-start.7 = ((f32[16,14,128]{2,1,0:T(8,128)}), f32[16,14,128]{2,1,0:T(8,128)S(1)}, u32[]{:S(2)}, u32[]{:S(2)}) async-start(f32[16,14,128]{2,1,0:T(8,128)} %broadcast_in_dim.8), calls=%async_computation.7 | async-start | bytes 262144 | tf_op jit(solution)/shard_map/all_to_all | solution.py:255
  218.2 11.5 %copy-start.8 = (f32[256,1024]{1,0:T(8,128)S(1)}, f32[256,1024]{1,0:T(8,128)}, u32[]{:S(2)}) copy-start(f32[256,1024]{1,0:T(8,128)} %get-tuple-element.274) | copy-start | bytes 3145732
  (7 other events, 9.5 us)
Sparse Core Ops, SparseCore 0:
  115.9 101.9 all-reduce.9
